TPU v7x, 128 devices: a whole 4x4x4 slice. The times are simulated.
128 devices in a mesh: kv: 16 (over y, x), seq: 8 (over z, core).
Axes of the slice: x: 4, y: 4, z: 4, core: 2. Of those that a mesh axis runs over, the one named last changes fastest.
Arguments:
- prefill_keys: bfloat16 [262144, 1024], P(('kv', 'seq')), may hold values from -50 to 50
- queries: bfloat16 [1024, 8192], P('seq'), may hold values from -6 to 6
- outlier_spans: int32 [512], P(('kv', 'seq')), may hold values from 0 to 255
- start_basis: float32 [160, 1024], replicated, may hold values from -6 to 6
Outputs:
- basis: float32 [160, 1024], replicated
- coefficients: bfloat16 [160, 262144], P(None, ('kv', 'seq'))
- landmark_scores: bfloat16 [8, 1024, 32768], P(None, 'seq', 'kv')
- outlier_scores: bfloat16 [8, 1024, 4096], P(None, 'seq', 'kv')
Inputs may be any that keep to these rules, and one draw needn't show every extreme that they name: `outlier_spans`: entries index spans of 8 rows among the rows held by the same device.
All inputs are finite; a program needn't handle non-finite values.
Results may differ from a plain program's by a relative error of at most 0.0037.
Values may be sent and summed in bfloat16 or wider, within the bound.
No kernel may reach another device: no remote copies, remote signals or barrier semaphores. Data moves between devices by JAX's collectives and lax.ppermute only.
A program may use at most 128 MiB of HBM per device.

v0:
```python
import math
import jax
import jax.numpy as jnp
from jax import lax
from jax.sharding import PartitionSpec as P

KVH = 8
HEAD = 128
GROUP = 8
ITERS = 8
SPAN = 8


def moment_of(product):
    return jnp.dot(
        product, product.T, precision=lax.Precision.HIGHEST, preferred_element_type=jnp.float32
    )


def solve_lower(moment, product):
    return jax.scipy.linalg.solve_triangular(jnp.linalg.cholesky(moment), product, lower=True)


def apply_gram(subspace, gram_rows):
    return lax.dot_general(
        subspace,
        gram_rows,
        (((1,), (1,)), ((), ())),
        precision=lax.Precision.HIGHEST,
        preferred_element_type=jnp.float32,
    )


def local(prefill_keys, queries, outlier_spans, start_basis):
    rows_dev = prefill_keys.shape[0]
    width = prefill_keys.shape[1]
    inverse_tokens = 1.0 / (rows_dev * lax.axis_size("kv") * lax.axis_size("seq"))
    scale_factor = 1.0 / math.sqrt(HEAD)
    spanned = prefill_keys.reshape(rows_dev // SPAN, SPAN, width)
    landmarks = jnp.mean(spanned, axis=1, dtype=jnp.float32).astype(jnp.bfloat16)
    picked = jnp.take(spanned, outlier_spans, axis=0).reshape(-1, width)
    query_count = queries.shape[0]
    query_heads = jnp.transpose(queries.reshape(query_count, KVH, GROUP, HEAD), (1, 0, 2, 3))

    def score_rows(shard_rows):
        count_rows = shard_rows.shape[0]
        key_heads = jnp.swapaxes(shard_rows.reshape(count_rows, KVH, HEAD), 0, 1)

        def one_head(pairing):
            query_group, key_group = pairing
            scores = jnp.einsum(
                "qgd,cd->qgc", query_group, key_group, preferred_element_type=jnp.float32
            )
            return jnp.max(scores, axis=1)

        return (lax.map(one_head, (query_heads, key_heads)) * scale_factor).astype(jnp.bfloat16)

    landmark_scores = score_rows(lax.all_gather(landmarks, "seq", axis=0, tiled=True))
    outlier_scores = score_rows(lax.all_gather(picked, "seq", axis=0, tiled=True))
    subspace = start_basis
    gram_block = lax.psum_scatter(
        lax.dot_general(
            prefill_keys, prefill_keys, (((0,), (0,)), ((), ())), preferred_element_type=jnp.float32
        )
        * inverse_tokens,
        "kv",
        scatter_dimension=0,
        tiled=True,
    )
    gram_rows = lax.psum(gram_block, "seq")
    for iteration in range(ITERS):
        product = apply_gram(subspace, gram_rows)
        moment = lax.psum(moment_of(product), "kv")
        basis_piece = solve_lower(moment, product)
        subspace = lax.all_gather(basis_piece, "kv", axis=1, tiled=True)
    rounded = subspace.astype(jnp.bfloat16)
    coefficients = lax.dot_general(
        rounded, prefill_keys, (((1,), (1,)), ((), ())), preferred_element_type=jnp.float32
    ).astype(jnp.bfloat16)
    return (subspace, coefficients, landmark_scores, outlier_scores)


def solution(mesh):
    placed = (P(("kv", "seq"), None), P("seq", None), P(("kv", "seq")), P())
    return jax.shard_map(
        local,
        mesh=mesh,
        in_specs=placed,
        out_specs=(P(), P(None, ("kv", "seq")), P(None, "seq", "kv"), P(None, "seq", "kv")),
        check_vma=False,
    )
```

profile of v0, /device:TPU:0, one launch (start us, length us, event | category | flops | bytes accessed | tf_op | source)
XLA Modules:
  0.0 1433.7 jit_solution(11385063445946750643)
XLA Ops:
  17.4 80.1 %reduce-scatter.2.cloned.1.call-done = f32[64,1024]{1,0:T(8,128)} async-done(((f32[1024,1024]{1,0:T(8,128)}), f32[64,1024]{1,0:T(8,128)}) %reduce-scatter.2.cloned.1.call-update) | async-done | bytes 262160 | tf_op jit(solution)/shard_map/reduce_scatter | solution.py:61
  97.5 61.8 %all-reduce.13.cloned.1.call-done = f32[64,1024]{1,0:T(8,128)} async-done(((f32[64,1024]{1,0:T(8,128)}), f32[64,1024]{1,0:T(8,128)}) %all-reduce.13.cloned.1.call-update) | async-done | bytes 262160 | tf_op jit(solution)/shard_map/psum | solution.py:70
  162.7 82.6 %all-reduce.15.cloned.1.call-done = f32[160,160]{0,1:T(8,128)} async-done(((f32[160,160]{0,1:T(8,128)}), f32[160,160]{0,1:T(8,128)}) %all-reduce.15.cloned.1.call-update) | async-done | bytes 102416 | tf_op jit(solution)/shard_map/psum | solution.py:73
  274.9 19.7 %custom-call.26 = f32[2,128,128]{1,2,0:T(8,128)S(1)} custom-call(f32[2,128,128]{2,1,0:T(8,128)S(1)} %pad_maximum_fusion), custom_call_target="InvertDiagBlocksLowerTriangular" | custom-call | tf_op jit(solution)/shard_map/jit(_solve_triangular)/triangular_solve | solution.py:21
  295.1 23.2 %all_gather.30 = f32[160,1024]{0,1:T(8,128)S(1)} all-gather(f32[160,64]{0,1:T(8,128)S(1)} %pad_maximum_fusion.8), channel_id=1, replica_groups=mesh['kv'=16,'seq'=8] {'kv'}, dimensions={1}, use_global_device_ids=true | all-gather | bytes 696320 | tf_op jit(solution)/shard_map/all_gather | solution.py:75
  320.3 82.5 %all-reduce.17.cloned.1.call-done = f32[160,160]{0,1:T(8,128)} async-done(((f32[160,160]{0,1:T(8,128)}), f32[160,160]{0,1:T(8,128)}) %all-reduce.17.cloned.1.call-update) | async-done | bytes 102416 | tf_op jit(solution)/shard_map/psum | solution.py:73
  432.4 19.7 %custom-call.28 = f32[2,128,128]{1,2,0:T(8,128)S(1)} custom-call(f32[2,128,128]{2,1,0:T(8,128)S(1)} %pad_maximum_fusion.1), custom_call_target="InvertDiagBlocksLowerTriangular" | custom-call | tf_op jit(solution)/shard_map/jit(_solve_triangular)/triangular_solve | solution.py:21
  452.6 23.2 %all_gather.31 = f32[160,1024]{0,1:T(8,128)S(1)} all-gather(f32[160,64]{0,1:T(8,128)S(1)} %pad_maximum_fusion.9), channel_id=1, replica_groups=mesh['kv'=16,'seq'=8] {'kv'}, dimensions={1}, use_global_device_ids=true | all-gather | bytes 696320 | tf_op jit(solution)/shard_map/all_gather | solution.py:75
  478.0 82.3 %all-reduce.19.cloned.1.call-done = f32[160,160]{0,1:T(8,128)} async-done(((f32[160,160]{0,1:T(8,128)}), f32[160,160]{0,1:T(8,128)}) %all-reduce.19.cloned.1.call-update) | async-done | bytes 102416 | tf_op jit(solution)/shard_map/psum | solution.py:73
  589.8 19.7 %custom-call.30 = f32[2,128,128]{1,2,0:T(8,128)S(1)} custom-call(f32[2,128,128]{2,1,0:T(8,128)S(1)} %pad_maximum_fusion.2), custom_call_target="InvertDiagBlocksLowerTriangular" | custom-call | tf_op jit(solution)/shard_map/jit(_solve_triangular)/triangular_solve | solution.py:21
  610.1 23.2 %all_gather.32 = f32[160,1024]{0,1:T(8,128)S(1)} all-gather(f32[160,64]{0,1:T(8,128)S(1)} %pad_maximum_fusion.10), channel_id=1, replica_groups=mesh['kv'=16,'seq'=8] {'kv'}, dimensions={1}, use_global_device_ids=true | all-gather | bytes 696320 | tf_op jit(solution)/shard_map/all_gather | solution.py:75
  640.7 77.0 %all-reduce.21.cloned.1.call-done = f32[160,160]{0,1:T(8,128)} async-done(((f32[160,160]{0,1:T(8,128)}), f32[160,160]{0,1:T(8,128)}) %all-reduce.21.cloned.1.call-update) | async-done | bytes 102416 | tf_op jit(solution)/shard_map/psum | solution.py:73
  747.3 19.7 %custom-call.32 = f32[2,128,128]{1,2,0:T(8,128)S(1)} custom-call(f32[2,128,128]{2,1,0:T(8,128)S(1)} %pad_maximum_fusion.3), custom_call_target="InvertDiagBlocksLowerTriangular" | custom-call | tf_op jit(solution)/shard_map/jit(_solve_triangular)/triangular_solve | solution.py:21
  767.5 23.2 %all_gather.33 = f32[160,1024]{0,1:T(8,128)S(1)} all-gather(f32[160,64]{0,1:T(8,128)S(1)} %pad_maximum_fusion.11), channel_id=1, replica_groups=mesh['kv'=16,'seq'=8] {'kv'}, dimensions={1}, use_global_device_ids=true | all-gather | bytes 696320 | tf_op jit(solution)/shard_map/all_gather | solution.py:75
  832.0 43.2 %all-reduce.23.cloned.1.call-done = f32[160,160]{0,1:T(8,128)} async-done(((f32[160,160]{0,1:T(8,128)}), f32[160,160]{0,1:T(8,128)}) %all-reduce.23.cloned.1.call-update) | async-done | bytes 102416 | tf_op jit(solution)/shard_map/psum | solution.py:73
  904.8 19.7 %custom-call.34 = f32[2,128,128]{1,2,0:T(8,128)S(1)} custom-call(f32[2,128,128]{2,1,0:T(8,128)S(1)} %pad_maximum_fusion.4), custom_call_target="InvertDiagBlocksLowerTriangular" | custom-call | tf_op jit(solution)/shard_map/jit(_solve_triangular)/triangular_solve | solution.py:21
  925.0 23.2 %all_gather.34 = f32[160,1024]{0,1:T(8,128)S(1)} all-gather(f32[160,64]{0,1:T(8,128)S(1)} %pad_maximum_fusion.12), channel_id=1, replica_groups=mesh['kv'=16,'seq'=8] {'kv'}, dimensions={1}, use_global_device_ids=true | all-gather | bytes 696320 | tf_op jit(solution)/shard_map/all_gather | solution.py:75
  957.5 75.2 %all-reduce.25.cloned.1.call-done = f32[160,160]{0,1:T(8,128)} async-done(((f32[160,160]{0,1:T(8,128)}), f32[160,160]{0,1:T(8,128)}) %all-reduce.25.cloned.1.call-update) | async-done | bytes 102416 | tf_op jit(solution)/shard_map/psum | solution.py:73
  1082.5 23.2 %all_gather.35 = f32[160,1024]{0,1:T(8,128)S(1)} all-gather(f32[160,64]{0,1:T(8,128)S(1)} %pad_maximum_fusion.13), channel_id=1, replica_groups=mesh['kv'=16,'seq'=8] {'kv'}, dimensions={1}, use_global_device_ids=true | all-gather | bytes 696320 | tf_op jit(solution)/shard_map/all_gather | solution.py:75
  1107.5 28.5 %while.29 = (s32[]{:T(128)}, f32[8,128,2048]{2,1,0:T(8,128)}, bf16[8,128,8,128]{3,1,2,0:T(8,128)(2,1)}, bf16[8,2048,128]{1,2,0:T(8,128)(2,1)}, s32[]{:T(128)}) while((s32[]{:T(128)}, f32[8,128,2048]{2,1,0:T(8,128)}, bf16[8,128,8,128]{3,1,2,0:T(8,128)(2,1)}, bf16[8,2048,128]{1,2,0:T(8,128)(2,1)}, s32[]{:T(128)}) %tuple.132), condition=%wide.region_17.20_spmd, body=%wide.region_15.19_spmd.sunk | while | flops 538705920 | bytes 3933757 | solution.py:56
  1136.0 54.1 %all-reduce.27.cloned.1.call-done = f32[160,160]{0,1:T(8,128)} async-done(((f32[160,160]{0,1:T(8,128)}), f32[160,160]{0,1:T(8,128)}) %all-reduce.27.cloned.1.call-update) | async-done | bytes 102416 | tf_op jit(solution)/shard_map/psum | solution.py:73
  1239.9 23.4 %all_gather.36 = f32[160,1024]{0,1:T(8,128)S(1)} all-gather(f32[160,64]{0,1:T(8,128)S(1)} %pad_maximum_fusion.14), channel_id=1, replica_groups=mesh['kv'=16,'seq'=8] {'kv'}, dimensions={1}, use_global_device_ids=true | all-gather | bytes 696320 | tf_op jit(solution)/shard_map/all_gather | solution.py:75
  1271.7 76.1 %all-reduce.29.cloned.1.call-done = f32[160,160]{0,1:T(8,128)} async-done(((f32[160,160]{0,1:T(8,128)}), f32[160,160]{0,1:T(8,128)}) %all-reduce.29.cloned.1.call-update) | async-done | bytes 102416 | tf_op jit(solution)/shard_map/psum | solution.py:73
  1397.7 23.3 %all_gather.37 = f32[160,1024]{0,1:T(8,128)S(1)} all-gather(f32[160,64]{0,1:T(8,128)S(1)} %pad_maximum_fusion.15), channel_id=1, replica_groups=mesh['kv'=16,'seq'=8] {'kv'}, dimensions={1}, use_global_device_ids=true | all-gather | bytes 696320 | tf_op jit(solution)/shard_map/all_gather | solution.py:75
  (283 shorter events, 423.8 us)
Async XLA Ops:
  7.2 152.2 %copy-start = (f32[160,1024]{1,0:T(8,128)S(1)}, f32[160,1024]{1,0:T(8,128)}, u32[]{:S(2)}) copy-start(f32[160,1024]{1,0:T(8,128)} %param.14) | copy-start | bytes 1966084
  7.2 90.3 %reduce-scatter.2.cloned.1.call-start = ((), (), s32[]{:S(2)}) async-start(), calls=%async_computation.1 | async-start | bytes 4456448 | tf_op jit(solution)/shard_map/reduce_scatter | solution.py:61
  17.3 142.0 %all-reduce.13.cloned.1.call-start = ((), (), s32[]{:S(2)}) async-start(), calls=%async_computation.2 | async-start | bytes 524288 | tf_op jit(solution)/shard_map/psum | solution.py:70
  97.5 147.9 %all-reduce.15.cloned.1.call-start = ((), (), s32[]{:S(2)}) async-start(), calls=%async_computation.3 | async-start | bytes 327680 | tf_op jit(solution)/shard_map/psum | solution.py:73
  159.4 159.0 %copy-start.2 = (f32[64,1024]{1,0:T(8,128)S(1)}, f32[64,1024]{1,0:T(8,128)}, u32[]{:S(2)}) copy-start(f32[64,1024]{1,0:T(8,128)} %all-reduce.13.cloned.1.call-done) | copy-start | bytes 786436
  162.2 240.6 %all-reduce.17.cloned.1.call-start = ((), (), s32[]{:S(2)}) async-start(), calls=%async_computation.4 | async-start | bytes 327680 | tf_op jit(solution)/shard_map/psum | solution.py:73
  320.1 240.2 %all-reduce.19.cloned.1.call-start = ((), (), s32[]{:S(2)}) async-start(), calls=%async_computation.5 | async-start | bytes 327680 | tf_op jit(solution)/shard_map/psum | solution.py:73
  477.6 240.2 %all-reduce.21.cloned.1.call-start = ((), (), s32[]{:S(2)}) async-start(), calls=%async_computation.6 | async-start | bytes 327680 | tf_op jit(solution)/shard_map/psum | solution.py:73
  635.0 240.2 %all-reduce.23.cloned.1.call-start = ((), (), s32[]{:S(2)}) async-start(), calls=%async_computation.7 | async-start | bytes 327680 | tf_op jit(solution)/shard_map/psum | solution.py:73
  792.5 158.4 %all-gather.2.cloned.1.call-start = ((), (), s32[]{:S(2)}) async-start(), calls=%async_computation.11 | async-start | bytes 4718592 | tf_op jit(solution)/shard_map/all_gather | solution.py:58
  793.4 239.2 %all-reduce.25.cloned.1.call-start = ((), (), s32[]{:S(2)}) async-start(), calls=%async_computation.8 | async-start | bytes 327680 | tf_op jit(solution)/shard_map/psum | solution.py:73
  793.5 5.9 copy-start.4
  832.0 118.0 %copy-start.3 = (f32[8,128,256]{2,1,0:T(8,128)S(1)}, f32[8,128,256]{2,1,0:T(8,128)}, u32[]{:S(2)}) copy-start(f32[8,128,256]{2,1,0:T(8,128)} %get-tuple-element.51) | copy-start | bytes 3145732
  949.9 240.2 %all-reduce.27.cloned.1.call-start = ((), (), s32[]{:S(2)}) async-start(), calls=%async_computation.9 | async-start | bytes 327680 | tf_op jit(solution)/shard_map/psum | solution.py:73
  1107.4 240.4 %all-reduce.29.cloned.1.call-start = ((), (), s32[]{:S(2)}) async-start(), calls=%async_computation.10 | async-start | bytes 327680 | tf_op jit(solution)/shard_map/psum | solution.py:73
  1397.7 29.0 %copy-start.1 = (f32[160,1024]{1,0:T(8,128)S(1)}, f32[160,1024]{1,0:T(8,128)}, u32[]{:S(2)}) copy-start(f32[160,1024]{1,0:T(8,128)} %param.14) | copy-start | bytes 1966084
Sparse Core Ops, SparseCore 0:
  17.5 79.9 reduce-scatter.1
  99.9 59.4 all-reduce.12
  163.2 82.1 all-reduce.14
  320.2 82.5 all-reduce.16
  477.7 82.5 all-reduce.18
  635.1 82.5 all-reduce.20
  792.6 82.5 all-reduce.22
  877.5 31.3 all-gather.1
  950.1 82.5 all-reduce.24
  1107.5 82.5 all-reduce.26
  1265.3 82.5 all-reduce.28
where the time goes:
time: 1440 us; the launch traced here: 1430 us
  waiting for transfers between devices  715 us (50%)
  other arithmetic  386 us (27%)
  blocking collectives  199 us (14%)
  matrix products  65.8 us (5%)
  local copies, waits for them, and re-layouts  39.1 us (3%)
  between operations  25.9 us (2%)
    psum x8, waiting for transfers between devices, local(): moment = lax.psum(moment_of(product), 'kv')  573 us
    another operation x56, other arithmetic, solve_lower(): jnp.linalg.cholesky(moment)  206 us
    all_gather x8, blocking collectives, local(): subspace = lax.all_gather(basis_piece, 'kv', axis=1, tiled=True)  186 us
    another operation x42, other arithmetic, solve_lower(): jax.scipy.linalg.solve_triangular(jnp.linalg.cholesky(moment), product, l...  158 us
    reduce_scatter x1, waiting for transfers between devices, local(): lax.psum_scatter(lax.dot_general(prefill_keys, prefill_keys, (((0,), (0,)...  80.1 us
    psum x1, waiting for transfers between devices, local(): gram_rows = lax.psum(gram_block, 'seq')  61.8 us
    dot_general x16, matrix products, one_head(): jnp.einsum('qgd,cd->qgc', query_group, key_group, preferred_element_type=...  29.6 us
  transfers between devices with their start and end apart: 11, of which 10 were waited for; matrix products, arithmetic and copies ran while one was open for 9% of the time, Pallas kernels for 0%

commit v1 on v0

--- a/solution.py
+++ b/solution.py
@@ -70,7 +70,9 @@
     gram_rows = lax.psum(gram_block, "seq")
     for iteration in range(ITERS):
         product = apply_gram(subspace, gram_rows)
-        moment = lax.psum(moment_of(product), "kv")
+        own = moment_of(product)
+        shards = lax.all_gather(own, "kv", axis=0, tiled=False)
+        moment = shards.sum(axis=0)
         basis_piece = solve_lower(moment, product)
         subspace = lax.all_gather(basis_piece, "kv", axis=1, tiled=True)
     rounded = subspace.astype(jnp.bfloat16)

time: 1440 us -> 1150 us (0.80)
  waiting for transfers between devices: 715 us -> 412 us
    psum x8 -> x0, waiting for transfers between devices: 573 us -> none  [local(): moment = lax.psum(moment_of(product), 'kv')]
    all_gather x0 -> x8, waiting for transfers between devices: none -> 270 us  [local(): shards = lax.all_gather(own, 'kv', axis=0, tiled=False)]
    reduce_sum x0 -> x8, other arithmetic: none -> 15.4 us  [local(): moment = shards.sum(axis=0)]
  transfers between devices with their start and end apart: 11 -> 11, of which waited for: 10 -> 9; matrix products, arithmetic and copies ran while one was open for 9% -> 11% of each run, Pallas kernels for 0% -> 0%
where the time goes in v1:
time: 1150 us; the launch traced here: 1140 us
  waiting for transfers between devices  412 us (36%)
  other arithmetic  395 us (34%)
  blocking collectives  209 us (18%)
  matrix products  65.8 us (6%)
  local copies, waits for them, and re-layouts  31.6 us (3%)
  between operations  25.7 us (2%)
    all_gather x8, waiting for transfers between devices, local(): shards = lax.all_gather(own, 'kv', axis=0, tiled=False)  270 us
    another operation x56, other arithmetic, solve_lower(): jnp.linalg.cholesky(moment)  206 us
    all_gather x8, blocking collectives, local(): subspace = lax.all_gather(basis_piece, 'kv', axis=1, tiled=True)  195 us
    another operation x42, other arithmetic, solve_lower(): jax.scipy.linalg.solve_triangular(jnp.linalg.cholesky(moment), product, l...  158 us
    reduce_scatter x1, waiting for transfers between devices, local(): lax.psum_scatter(lax.dot_general(prefill_keys, prefill_keys, (((0,), (0,)...  80.1 us
    psum x1, waiting for transfers between devices, local(): gram_rows = lax.psum(gram_block, 'seq')  61.9 us
    dot_general x16, matrix products, one_head(): jnp.einsum('qgd,cd->qgc', query_group, key_group, preferred_element_type=...  29.6 us
  transfers between devices with their start and end apart: 11, of which 9 were waited for; matrix products, arithmetic and copies ran while one was open for 11% of the time, Pallas kernels for 0%

profile of v1, /device:TPU:0, one launch (start us, length us, event | category | flops | bytes accessed | tf_op | source)
XLA Modules:
  0.0 1142.0 jit_solution(9140807122874861171)
XLA Ops:
  17.4 80.1 %reduce-scatter.2.cloned.1.call-done = f32[64,1024]{1,0:T(8,128)} async-done(((f32[1024,1024]{1,0:T(8,128)}), f32[64,1024]{1,0:T(8,128)}) %reduce-scatter.2.cloned.1.call-update) | async-done | bytes 262160 | tf_op jit(solution)/shard_map/reduce_scatter | solution.py:61
  97.5 61.9 %all-reduce.5.cloned.1.call-done = f32[64,1024]{1,0:T(8,128)} async-done(((f32[64,1024]{1,0:T(8,128)}), f32[64,1024]{1,0:T(8,128)}) %all-reduce.5.cloned.1.call-update) | async-done | bytes 262160 | tf_op jit(solution)/shard_map/psum | solution.py:70
  162.8 44.7 %all-gather.20.cloned.1.call-done = f32[2560,160]{1,0:T(8,128)} async-done(((f32[160,160]{1,0:T(8,128)}), f32[2560,160]{1,0:T(8,128)}) %all-gather.20.cloned.1.call-update) | async-done | bytes 1638416 | tf_op jit(solution)/shard_map/all_gather | solution.py:74
  237.2 19.7 %custom-call.26 = f32[2,128,128]{1,2,0:T(8,128)S(1)} custom-call(f32[2,128,128]{2,1,0:T(8,128)S(1)} %pad_maximum_fusion), custom_call_target="InvertDiagBlocksLowerTriangular" | custom-call | tf_op jit(solution)/shard_map/jit(_solve_triangular)/triangular_solve | solution.py:21
  257.4 24.6 %all_gather.80 = f32[160,1024]{0,1:T(8,128)S(1)} all-gather(f32[160,64]{0,1:T(8,128)S(1)} %pad_maximum_fusion.8), channel_id=1, replica_groups=mesh['kv'=16,'seq'=8] {'kv'}, dimensions={1}, use_global_device_ids=true | all-gather | bytes 696320 | tf_op jit(solution)/shard_map/all_gather | solution.py:77
  284.0 44.4 %all-gather.22.cloned.1.call-done = f32[2560,160]{1,0:T(8,128)} async-done(((f32[160,160]{1,0:T(8,128)}), f32[2560,160]{1,0:T(8,128)}) %all-gather.22.cloned.1.call-update) | async-done | bytes 1638416 | tf_op jit(solution)/shard_map/all_gather | solution.py:74
  358.1 19.7 %custom-call.28 = f32[2,128,128]{1,2,0:T(8,128)S(1)} custom-call(f32[2,128,128]{2,1,0:T(8,128)S(1)} %pad_maximum_fusion.1), custom_call_target="InvertDiagBlocksLowerTriangular" | custom-call | tf_op jit(solution)/shard_map/jit(_solve_triangular)/triangular_solve | solution.py:21
  378.3 24.6 %all_gather.83 = f32[160,1024]{0,1:T(8,128)S(1)} all-gather(f32[160,64]{0,1:T(8,128)S(1)} %pad_maximum_fusion.9), channel_id=1, replica_groups=mesh['kv'=16,'seq'=8] {'kv'}, dimensions={1}, use_global_device_ids=true | all-gather | bytes 696320 | tf_op jit(solution)/shard_map/all_gather | solution.py:77
  405.0 44.4 %all-gather.24.cloned.1.call-done = f32[2560,160]{1,0:T(8,128)} async-done(((f32[160,160]{1,0:T(8,128)}), f32[2560,160]{1,0:T(8,128)}) %all-gather.24.cloned.1.call-update) | async-done | bytes 1638416 | tf_op jit(solution)/shard_map/all_gather | solution.py:74
  479.0 19.7 %custom-call.30 = f32[2,128,128]{1,2,0:T(8,128)S(1)} custom-call(f32[2,128,128]{2,1,0:T(8,128)S(1)} %pad_maximum_fusion.2), custom_call_target="InvertDiagBlocksLowerTriangular" | custom-call | tf_op jit(solution)/shard_map/jit(_solve_triangular)/triangular_solve | solution.py:21
  499.3 24.6 %all_gather.86 = f32[160,1024]{0,1:T(8,128)S(1)} all-gather(f32[160,64]{0,1:T(8,128)S(1)} %pad_maximum_fusion.10), channel_id=1, replica_groups=mesh['kv'=16,'seq'=8] {'kv'}, dimensions={1}, use_global_device_ids=true | all-gather | bytes 696320 | tf_op jit(solution)/shard_map/all_gather | solution.py:77
  526.1 44.4 %all-gather.26.cloned.1.call-done = f32[2560,160]{1,0:T(8,128)} async-done(((f32[160,160]{1,0:T(8,128)}), f32[2560,160]{1,0:T(8,128)}) %all-gather.26.cloned.1.call-update) | async-done | bytes 1638416 | tf_op jit(solution)/shard_map/all_gather | solution.py:74
  600.1 19.7 %custom-call.32 = f32[2,128,128]{1,2,0:T(8,128)S(1)} custom-call(f32[2,128,128]{2,1,0:T(8,128)S(1)} %pad_maximum_fusion.3), custom_call_target="InvertDiagBlocksLowerTriangular" | custom-call | tf_op jit(solution)/shard_map/jit(_solve_triangular)/triangular_solve | solution.py:21
  620.4 24.6 %all_gather.89 = f32[160,1024]{0,1:T(8,128)S(1)} all-gather(f32[160,64]{0,1:T(8,128)S(1)} %pad_maximum_fusion.11), channel_id=1, replica_groups=mesh['kv'=16,'seq'=8] {'kv'}, dimensions={1}, use_global_device_ids=true | all-gather | bytes 696320 | tf_op jit(solution)/shard_map/all_gather | solution.py:77
  647.0 44.6 %all-gather.28.cloned.1.call-done = f32[2560,160]{1,0:T(8,128)} async-done(((f32[160,160]{1,0:T(8,128)}), f32[2560,160]{1,0:T(8,128)}) %all-gather.28.cloned.1.call-update) | async-done | bytes 1638416 | tf_op jit(solution)/shard_map/all_gather | solution.py:74
  721.3 19.7 %custom-call.34 = f32[2,128,128]{1,2,0:T(8,128)S(1)} custom-call(f32[2,128,128]{2,1,0:T(8,128)S(1)} %pad_maximum_fusion.4), custom_call_target="InvertDiagBlocksLowerTriangular" | custom-call | tf_op jit(solution)/shard_map/jit(_solve_triangular)/triangular_solve | solution.py:21
  741.5 24.6 %all_gather.92 = f32[160,1024]{0,1:T(8,128)S(1)} all-gather(f32[160,64]{0,1:T(8,128)S(1)} %pad_maximum_fusion.12), channel_id=1, replica_groups=mesh['kv'=16,'seq'=8] {'kv'}, dimensions={1}, use_global_device_ids=true | all-gather | bytes 696320 | tf_op jit(solution)/shard_map/all_gather | solution.py:77
  774.7 38.0 %all-gather.30.cloned.1.call-done = f32[2560,160]{1,0:T(8,128)} async-done(((f32[160,160]{1,0:T(8,128)}), f32[2560,160]{1,0:T(8,128)}) %all-gather.30.cloned.1.call-update) | async-done | bytes 1638416 | tf_op jit(solution)/shard_map/all_gather | solution.py:74
  842.4 19.7 %custom-call.36 = f32[2,128,128]{1,2,0:T(8,128)S(1)} custom-call(f32[2,128,128]{2,1,0:T(8,128)S(1)} %pad_maximum_fusion.5), custom_call_target="InvertDiagBlocksLowerTriangular" | custom-call | tf_op jit(solution)/shard_map/jit(_solve_triangular)/triangular_solve | solution.py:21
  862.6 24.4 %all_gather.95 = f32[160,1024]{0,1:T(8,128)S(1)} all-gather(f32[160,64]{0,1:T(8,128)S(1)} %pad_maximum_fusion.13), channel_id=1, replica_groups=mesh['kv'=16,'seq'=8] {'kv'}, dimensions={1}, use_global_device_ids=true | all-gather | bytes 696320 | tf_op jit(solution)/shard_map/all_gather | solution.py:77
  965.3 19.7 %custom-call.38 = f32[2,128,128]{1,2,0:T(8,128)S(1)} custom-call(f32[2,128,128]{2,1,0:T(8,128)S(1)} %pad_maximum_fusion.6), custom_call_target="InvertDiagBlocksLowerTriangular" | custom-call | tf_op jit(solution)/shard_map/jit(_solve_triangular)/triangular_solve | solution.py:21
  985.6 22.7 %all_gather.98 = f32[160,1024]{0,1:T(8,128)S(1)} all-gather(f32[160,64]{0,1:T(8,128)S(1)} %pad_maximum_fusion.14), channel_id=1, replica_groups=mesh['kv'=16,'seq'=8] {'kv'}, dimensions={1}, use_global_device_ids=true | all-gather | bytes 696320 | tf_op jit(solution)/shard_map/all_gather | solution.py:77
  1010.1 28.5 %while.29 = (s32[]{:T(128)}, f32[8,128,2048]{2,1,0:T(8,128)}, bf16[8,128,8,128]{3,1,2,0:T(8,128)(2,1)}, bf16[8,2048,128]{1,2,0:T(8,128)(2,1)}, s32[]{:T(128)}) while((s32[]{:T(128)}, f32[8,128,2048]{2,1,0:T(8,128)}, bf16[8,128,8,128]{3,1,2,0:T(8,128)(2,1)}, bf16[8,2048,128]{1,2,0:T(8,128)(2,1)}, s32[]{:T(128)}) %tuple.132), condition=%wide.region_17.20_spmd, body=%wide.region_15.19_spmd.sunk | while | flops 538705920 | bytes 3933757 | solution.py:56
  1104.8 24.7 %all_gather.101 = f32[160,1024]{0,1:T(8,128)S(1)} all-gather(f32[160,64]{0,1:T(8,128)S(1)} %pad_maximum_fusion.15), channel_id=1, replica_groups=mesh['kv'=16,'seq'=8] {'kv'}, dimensions={1}, use_global_device_ids=true | all-gather | bytes 696320 | tf_op jit(solution)/shard_map/all_gather | solution.py:77
  (289 shorter events, 396.5 us)
Async XLA Ops:
  7.2 152.2 %copy-start = (f32[160,1024]{1,0:T(8,128)S(1)}, f32[160,1024]{1,0:T(8,128)}, u32[]{:S(2)}) copy-start(f32[160,1024]{1,0:T(8,128)} %param.14) | copy-start | bytes 1966084
  7.2 90.3 %reduce-scatter.2.cloned.1.call-start = ((), (), s32[]{:S(2)}) async-start(), calls=%async_computation.1 | async-start | bytes 4456448 | tf_op jit(solution)/shard_map/reduce_scatter | solution.py:61
  17.3 142.0 %all-reduce.5.cloned.1.call-start = ((), (), s32[]{:S(2)}) async-start(), calls=%async_computation.2 | async-start | bytes 524288 | tf_op jit(solution)/shard_map/psum | solution.py:70
  97.5 110.1 %all-gather.20.cloned.1.call-start = ((), (), s32[]{:S(2)}) async-start(), calls=%async_computation.4 | async-start | bytes 2785280 | tf_op jit(solution)/shard_map/all_gather | solution.py:74
  159.4 122.6 %copy-start.2 = (f32[64,1024]{1,0:T(8,128)S(1)}, f32[64,1024]{1,0:T(8,128)}, u32[]{:S(2)}) copy-start(f32[64,1024]{1,0:T(8,128)} %all-reduce.5.cloned.1.call-done) | copy-start | bytes 786436
  162.2 166.2 %all-gather.22.cloned.1.call-start = ((), (), s32[]{:S(2)}) async-start(), calls=%async_computation.5 | async-start | bytes 2785280 | tf_op jit(solution)/shard_map/all_gather | solution.py:74
  283.8 165.5 %all-gather.24.cloned.1.call-start = ((), (), s32[]{:S(2)}) async-start(), calls=%async_computation.6 | async-start | bytes 2785280 | tf_op jit(solution)/shard_map/all_gather | solution.py:74
  404.7 165.7 %all-gather.26.cloned.1.call-start = ((), (), s32[]{:S(2)}) async-start(), calls=%async_computation.7 | async-start | bytes 2785280 | tf_op jit(solution)/shard_map/all_gather | solution.py:74
  525.6 165.9 %all-gather.28.cloned.1.call-start = ((), (), s32[]{:S(2)}) async-start(), calls=%async_computation.8 | async-start | bytes 2785280 | tf_op jit(solution)/shard_map/all_gather | solution.py:74
  646.7 165.9 %all-gather.30.cloned.1.call-start = ((), (), s32[]{:S(2)}) async-start(), calls=%async_computation.9 | async-start | bytes 2785280 | tf_op jit(solution)/shard_map/all_gather | solution.py:74
  767.8 161.4 %all-gather.18.cloned.1.call-start = ((), (), s32[]{:S(2)}) async-start(), calls=%async_computation.3 | async-start | bytes 4718592 | tf_op jit(solution)/shard_map/all_gather | solution.py:58
  774.3 161.4 %all-gather.32.cloned.1.call-start = ((), (), s32[]{:S(2)}) async-start(), calls=%async_computation.10 | async-start | bytes 2785280 | tf_op jit(solution)/shard_map/all_gather | solution.py:74
  812.7 76.1 %copy-start.3 = (s32[4]{0:T(128)S(1)}, s32[4]{0:T(128)}, u32[]{:S(2)}) copy-start(s32[4]{0:T(128)} %param.13) | copy-start | bytes 52
  888.7 166.2 %all-gather.34.cloned.1.call-start = ((), (), s32[]{:S(2)}) async-start(), calls=%async_computation.11 | async-start | bytes 2785280 | tf_op jit(solution)/shard_map/all_gather | solution.py:74
  1104.8 30.4 %copy-start.1 = (f32[160,1024]{1,0:T(8,128)S(1)}, f32[160,1024]{1,0:T(8,128)}, u32[]{:S(2)}) copy-start(f32[160,1024]{1,0:T(8,128)} %param.14) | copy-start | bytes 1966084
Sparse Core Ops, SparseCore 0:
  17.5 79.9 reduce-scatter.1
  99.9 59.4 all-reduce.4
  162.4 45.1 all-gather.19
  283.9 44.4 all-gather.21
  404.8 44.4 all-gather.23
  525.7 44.6 all-gather.25
  646.8 44.6 all-gather.27
  768.0 44.6 all-gather.29
  815.0 31.8 all-gather.17
  888.9 44.7 all-gather.31
  1010.2 44.6 all-gather.33
